TPU v7x, 256 devices: a whole 4x4x8 slice. The times are simulated.
256 devices in a mesh: dp: 32 (over z, x_hi, core), tm: 8 (over y, x_lo).
Axes of the slice: x: 4 (x_hi: 2, x_lo: 2; x = x_hi * 2 + x_lo), y: 4, z: 8, core: 2. Of those that a mesh axis runs over, the one named last changes fastest.
Arguments:
- queries: bfloat16 [32, 3072, 256], P('dp', 'tm'), may hold values from -6 to 6
- key_input: bfloat16 [32, 3072, 256], P('dp', 'tm'), may hold values from -6 to 6
- value_input: bfloat16 [32, 3072, 256], P('dp', 'tm'), may hold values from -6 to 6
- lengths: int32 [32], P('dp'), may hold values from 1536 to 3072, as said below
- projection: bfloat16 [4096, 256], P('dp'), may hold values from -0.09375 to 0.09375
- upstream: bfloat16 [32, 3072, 4096], P('dp', 'tm'), may hold values from -6 to 6
- glu_input: bfloat16 [32, 3072, 4096], P('dp', 'tm'), may hold values from -6 to 6
- kernel: bfloat16 [2048, 31], P('dp'), may hold values from -1 to 1
- norm_gain: bfloat16 [2048], P('dp'), may hold values from 0.5 to 1.5
- conv_upstream: bfloat16 [32, 3072, 2048], P('dp', 'tm'), may hold values from -6 to 6
Outputs:
- grad_queries: bfloat16 [32, 3072, 256], P('dp', 'tm')
- grad_keys: bfloat16 [32, 3072, 256], P('dp', 'tm')
- grad_values: bfloat16 [32, 3072, 256], P('dp', 'tm')
- grad_projection: bfloat16 [4096, 256], P('dp')
- grad_glu: bfloat16 [32, 3072, 4096], P('dp', 'tm')
- grad_kernel: float32 [2048, 31], P('dp')
- grad_gain: float32 [2048], P('dp')
Inputs may be any that keep to these rules, and one draw needn't show every extreme that they name: `lengths`: the valid frames of an utterance are its first ones; one utterance has all 3072 valid and one exactly 1536.
All inputs are finite; a program needn't handle non-finite values.
Results may differ from a plain program's by a relative error of at most 0.02.
Values may be sent and summed in bfloat16 or wider, within the bound.
No kernel may reach another device: no remote copies, remote signals or barrier semaphores. Data moves between devices by JAX's collectives and lax.ppermute only.
A program may use at most 128 MiB of HBM per device.

v0:
```python
import jax
import jax.numpy as jnp
from jax import lax
from jax.sharding import PartitionSpec as P

HEADS = 2
HDIM = 128
CH = 2048
KW = 31
NEG_FILL = -1e30
NORM_EPS = 1e-05


def from_behind(block, axis, distance):
    devices = range(lax.axis_size(axis))
    route = [((i - distance) % len(devices), i) for i in devices]
    return lax.ppermute(block, axis, route)


def extended(cells, sides, width):
    for axis, dim in sides:
        count = lax.axis_size(axis)
        ends = count - 1
        head = lax.slice_in_dim(cells, 0, width, axis=dim)
        tail = lax.slice_in_dim(cells, cells.shape[dim] - width, cells.shape[dim], axis=dim)
        cells = jnp.concatenate(
            [
                lax.ppermute(tail, axis, [(i, (i + 1) % count) for i in range(ends)]),
                cells,
                lax.ppermute(head, axis, [((i + 1) % count, i) for i in range(ends)]),
            ],
            axis=dim,
        )
    return cells


def depthwise(padded, kernel_f, frame_rows):
    mixed = jnp.zeros((frame_rows, kernel_f.shape[0]), jnp.float32)
    for tap in range(kernel_f.shape[1]):
        mixed = mixed + padded[tap : tap + frame_rows].astype(jnp.float32) * kernel_f[:, tap]
    return mixed


def back_depthwise(grad_pad, kernel_f, frame_rows):
    half_width = (kernel_f.shape[1] - 1) // 2
    result = jnp.zeros((frame_rows, kernel_f.shape[0]), jnp.float32)
    for tap in range(kernel_f.shape[1]):
        begin = 2 * half_width - tap
        result = (
            result + grad_pad[begin : begin + frame_rows].astype(jnp.float32) * kernel_f[:, tap]
        )
    return result


def tap_products(grad_low, padded, frame_rows, tap_count):
    grad_f = grad_low.astype(jnp.float32)
    return jnp.stack(
        [
            jnp.sum(grad_f * padded[tap : tap + frame_rows].astype(jnp.float32), axis=0)
            for tap in range(tap_count)
        ],
        axis=1,
    )


def norm_backward(mixed, gain_f, cotangent, frame_live):
    centre = mixed - jnp.mean(mixed, axis=-1, keepdims=True)
    inv_std = lax.rsqrt(jnp.mean(centre * centre, axis=-1, keepdims=True) + NORM_EPS)
    standard = centre * inv_std
    normed = standard * gain_f
    squash = jax.nn.sigmoid(normed)
    grad_normed = (
        cotangent.astype(jnp.float32) * frame_live * (squash + normed * squash * (1.0 - squash))
    )
    gain_term = jnp.sum(grad_normed * standard, axis=0)
    scaled = grad_normed * gain_f
    grad_conv = inv_std * (
        scaled
        - jnp.mean(scaled, axis=-1, keepdims=True)
        - standard * jnp.mean(scaled * standard, axis=-1, keepdims=True)
    )
    return (grad_conv.astype(jnp.bfloat16), gain_term)


def gather_params(projection, kernel, norm_gain):
    width = projection.shape[1]
    tail = jnp.concatenate([kernel.reshape(-1), norm_gain.reshape(-1)])
    tail_rows = -(-tail.shape[0] // width)
    tail = jnp.pad(tail, (0, tail_rows * width - tail.shape[0])).reshape(tail_rows, width)
    block = jnp.concatenate([projection, tail], axis=0)
    full = lax.all_gather(block, "dp", axis=0, tiled=False)
    count = full.shape[0]
    proj_rows = projection.shape[0]
    full_proj = full[:, :proj_rows].reshape(count * proj_rows, width)
    flat_tail = full[:, proj_rows:].reshape(count, tail_rows * width)
    kernel_size = kernel.shape[0] * kernel.shape[1]
    full_kernel = flat_tail[:, :kernel_size].reshape(count * kernel.shape[0], kernel.shape[1])
    full_gain = flat_tail[:, kernel_size : kernel_size + norm_gain.shape[0]].reshape(-1)
    return (full_proj, full_kernel, full_gain)


def reduce_grads(proj_term, kernel_term, gain_term):
    count = lax.axis_size("dp")
    width = proj_term.shape[1]
    proj_part = lax.psum_scatter(proj_term, "dp", scatter_dimension=0, tiled=True)
    kernel_blocks = kernel_term.reshape(count, -1)
    gain_blocks = gain_term.reshape(count, -1)
    tail = jnp.concatenate([kernel_blocks, gain_blocks], axis=1)
    tail_cols = tail.shape[1]
    tail_rows = -(-tail_cols // width)
    tail = jnp.pad(tail, ((0, 0), (0, tail_rows * width - tail_cols))).reshape(-1, width)
    tail_part = lax.psum_scatter(tail, "dp", scatter_dimension=0, tiled=True)
    total = lax.psum(jnp.concatenate([proj_part, tail_part], axis=0), "tm")
    proj_rows = proj_part.shape[0]
    proj_total = total[:proj_rows]
    flat_tail = total[proj_rows:].reshape(-1)
    kernel_size = kernel_blocks.shape[1]
    kernel_total = flat_tail[:kernel_size].reshape(-1, kernel_term.shape[1])
    gain_total = flat_tail[kernel_size : kernel_size + gain_blocks.shape[1]]
    return (proj_total, kernel_total, gain_total)


def split_three(values):
    high = lax.optimization_barrier(values.astype(jnp.bfloat16))
    rest = values - high.astype(jnp.float32)
    middle = lax.optimization_barrier(rest.astype(jnp.bfloat16))
    low = (rest - middle.astype(jnp.float32)).astype(jnp.bfloat16)
    return jnp.concatenate([high, middle, low], axis=0)


def join_three(parts):
    third = parts.shape[0] // 3
    wide = parts.astype(jnp.float32)
    return wide[:third] + wide[third : 2 * third] + wide[2 * third :]


def per_device(
    queries,
    key_input,
    value_input,
    lengths,
    projection,
    upstream,
    glu_input,
    kernel,
    norm_gain,
    conv_upstream,
):
    time_count = lax.axis_size("tm")
    time_rank = lax.axis_index("tm")
    frame_rows = queries.shape[1]
    flat_width = queries.shape[2]
    score_scale = HDIM ** (-0.5)
    length = lengths[0]
    full_proj, full_kernel, full_gain = gather_params(projection, kernel, norm_gain)
    query_heads = queries[0].reshape(frame_rows, HEADS, HDIM)
    key_own = key_input[0].reshape(frame_rows, HEADS, HDIM)
    value_own = value_input[0].reshape(frame_rows, HEADS, HDIM)
    key_value = lax.all_gather(
        jnp.concatenate([key_input[0], value_input[0]], axis=1), "tm", axis=0, tiled=True
    )
    total_frames = key_value.shape[0]
    key_all = key_value[:, :flat_width].reshape(total_frames, HEADS, HDIM)
    value_all = key_value[:, flat_width:].reshape(total_frames, HEADS, HDIM)
    key_live = jnp.arange(total_frames, dtype=jnp.int32) < length
    scores = (
        jnp.einsum("qhd,khd->hqk", query_heads, key_all, preferred_element_type=jnp.float32)
        * score_scale
    )
    scores = jnp.where(key_live[None, None, :], scores, NEG_FILL)
    row_top = jnp.max(scores, axis=-1)
    log_total = row_top + jnp.log(jnp.sum(jnp.exp(scores - row_top[:, :, None]), axis=-1))
    weights = jnp.exp(scores - log_total[:, :, None])
    weights_high = lax.optimization_barrier(weights.astype(jnp.bfloat16))
    weights_rest = (weights - weights_high.astype(jnp.float32)).astype(jnp.bfloat16)
    attended = (
        jnp.einsum("hqk,khd->qhd", weights_high, value_all, preferred_element_type=jnp.float32)
        + jnp.einsum("hqk,khd->qhd", weights_rest, value_all, preferred_element_type=jnp.float32)
    ).astype(jnp.bfloat16)
    upstream_rows = upstream[0]
    grad_out = jnp.dot(upstream_rows, full_proj, preferred_element_type=jnp.float32).astype(
        jnp.bfloat16
    )
    grad_heads = grad_out.reshape(frame_rows, HEADS, HDIM)
    row_delta = jnp.einsum("qhd,qhd->hq", grad_heads, attended, preferred_element_type=jnp.float32)
    grad_weights = jnp.einsum(
        "qhd,khd->hqk", grad_heads, value_all, preferred_element_type=jnp.float32
    )
    grad_scores = (weights * (grad_weights - row_delta[:, :, None]) * score_scale).astype(
        jnp.bfloat16
    )
    query_acc = jnp.einsum("hqk,khd->qhd", grad_scores, key_all, preferred_element_type=jnp.float32)
    stat_parts = split_three(jnp.concatenate([log_total, row_delta], axis=0))
    pair_width = 2 * flat_width
    stat_rows = -(-stat_parts.size // pair_width)
    stat_rows = -(-stat_rows // 16) * 16
    stat_block = jnp.pad(stat_parts.reshape(-1), (0, stat_rows * pair_width - stat_parts.size))
    packed_rows = jnp.concatenate(
        [
            jnp.concatenate([queries[0], grad_out], axis=1),
            stat_block.reshape(stat_rows, pair_width),
        ],
        axis=0,
    )
    query_grad = lax.all_gather(packed_rows, "tm", axis=0, tiled=False)
    query_pairs = query_grad[:, :frame_rows].reshape(total_frames, pair_width)
    stat_all = query_grad[:, frame_rows:].reshape(time_count, -1)[:, : stat_parts.size]
    stat_all = stat_all.reshape(time_count, stat_parts.shape[0], frame_rows)
    stat_all = join_three(jnp.transpose(stat_all, (1, 0, 2)).reshape(stat_parts.shape[0], -1))
    query_all = query_pairs[:, :flat_width].reshape(total_frames, HEADS, HDIM)
    grad_all = query_pairs[:, flat_width:].reshape(total_frames, HEADS, HDIM)
    log_total_all = stat_all[:HEADS]
    row_delta_all = stat_all[HEADS:]
    own_live = time_rank * frame_rows + jnp.arange(frame_rows, dtype=jnp.int32) < length
    scores_k = (
        jnp.einsum("qhd,khd->hqk", query_all, key_own, preferred_element_type=jnp.float32)
        * score_scale
    )
    scores_k = jnp.where(own_live[None, None, :], scores_k, NEG_FILL)
    weights_k = jnp.exp(scores_k - log_total_all[:, :, None])
    value_acc = jnp.einsum(
        "hqk,qhd->khd", weights_k.astype(jnp.bfloat16), grad_all, preferred_element_type=jnp.float32
    )
    grad_weights_k = jnp.einsum(
        "qhd,khd->hqk", grad_all, value_own, preferred_element_type=jnp.float32
    )
    grad_scores_k = (weights_k * (grad_weights_k - row_delta_all[:, :, None]) * score_scale).astype(
        jnp.bfloat16
    )
    key_acc = jnp.einsum(
        "hqk,qhd->khd", grad_scores_k, query_all, preferred_element_type=jnp.float32
    )
    grad_queries = query_acc.reshape(1, frame_rows, flat_width).astype(jnp.bfloat16)
    grad_keys = key_acc.reshape(1, frame_rows, flat_width).astype(jnp.bfloat16)
    grad_values = value_acc.reshape(1, frame_rows, flat_width).astype(jnp.bfloat16)
    half_width = (KW - 1) // 2
    frame_ids = time_rank * frame_rows + jnp.arange(frame_rows, dtype=jnp.int32)
    frame_live = (frame_ids < length).astype(jnp.float32)[:, None]
    glu_rows = glu_input[0]
    linear = glu_rows[:, :CH].astype(jnp.float32)
    gate_sig = jax.nn.sigmoid(glu_rows[:, CH:].astype(jnp.float32))
    activ = (linear * gate_sig * frame_live).astype(jnp.bfloat16)
    padded = extended(activ, (("tm", 0),), half_width)
    kernel_f = full_kernel.astype(jnp.float32)
    gain_f = full_gain.astype(jnp.float32)
    mixed = depthwise(padded, kernel_f, frame_rows)
    grad_conv, gain_term = norm_backward(mixed, gain_f, conv_upstream[0], frame_live)
    grad_pad = extended(grad_conv, (("tm", 0),), half_width)
    kernel_term = tap_products(grad_conv, padded, frame_rows, KW)
    grad_activ = back_depthwise(grad_pad, kernel_f, frame_rows) * frame_live
    first_half = grad_activ * gate_sig
    second_half = grad_activ * linear * gate_sig * (1.0 - gate_sig)
    grad_glu = jnp.concatenate([first_half, second_half], axis=-1).astype(jnp.bfloat16)[None]
    attended_flat = attended.reshape(frame_rows, flat_width)
    proj_term = lax.dot_general(
        upstream_rows, attended_flat, (((0,), (0,)), ((), ())), preferred_element_type=jnp.float32
    )
    proj_total, kernel_total, gain_total = reduce_grads(proj_term, kernel_term, gain_term)
    grad_projection = proj_total.astype(jnp.bfloat16)
    return (
        grad_queries,
        grad_keys,
        grad_values,
        grad_projection,
        grad_glu,
        kernel_total,
        gain_total,
    )


def solution(mesh):
    in_specs = (
        P("dp", "tm", None),
        P("dp", "tm", None),
        P("dp", "tm", None),
        P("dp"),
        P("dp", None),
        P("dp", "tm", None),
        P("dp", "tm", None),
        P("dp", None),
        P("dp"),
        P("dp", "tm", None),
    )
    out_specs = (
        P("dp", "tm", None),
        P("dp", "tm", None),
        P("dp", "tm", None),
        P("dp", None),
        P("dp", "tm", None),
        P("dp", None),
        P("dp"),
    )
    return jax.shard_map(
        per_device, mesh=mesh, in_specs=in_specs, out_specs=out_specs, check_vma=False
    )
```

profile of v0, /device:TPU:4, one launch (start us, length us, event | category | flops | bytes accessed | tf_op | source)
XLA Modules:
  0.0 645.9 jit_solution(10095219337731439933)
XLA Ops:
  7.2 1.0 copy.85
  9.1 1.5 pad_maximum_fusion.9
  11.8 2.9 fusion.11
  14.8 1.2 copy-done.4
  16.7 1.3 collective-permute-start.1
  18.0 5.2 collective-permute-start
  23.2 1.7 copy.82
  25.7 1.8 pad_maximum_fusion.6
  29.2 62.8 %all-gather.8.cloned.1.call-done = bf16[4352,256]{1,0:T(8,128)(2,1)} async-done(((bf16[136,256]{1,0:T(8,128)(2,1)}), bf16[4352,256]{1,0:T(8,128)(2,1)}) %all-gather.8.cloned.1.call-update) | async-done | bytes 2228240 | tf_op jit(solution)/shard_map/all_gather | solution.py:91
  92.0 0.9 slice.619
  92.9 2.2 reshape.264
  95.2 19.6 %slice_reduce_fusion.30 = (f32[2048]{0:T(1024)S(1)}, f32[2048]{0:T(1024)S(1)}, f32[2048]{0:T(1024)S(1)}, f32[2048]{0:T(1024)S(1)}, f32[2048]{0:T(1024)S(1)}, /*i...) fusion(f32[2048,31]{1,0:T(8,128)} %reshape.264), kind=kLoop, calls=%fused_computation.353 | loop fusion | bytes 311296 | tf_op jit(solution)/shard_map/slice | solution.py:40
  114.9 6.6 %slice_reduce_fusion.29 = (f32[2048]{0:T(1024)S(1)}, f32[2048]{0:T(1024)S(1)}, f32[2048]{0:T(1024)S(1)}, f32[2048]{0:T(1024)S(1)}, f32[2048]{0:T(1024)S(1)}, /*i...) fusion(f32[2048,31]{1,0:T(8,128)S(1)} %copy-done.2), kind=kLoop, calls=%fused_computation.352 | loop fusion | bytes 196608 | tf_op jit(solution)/shard_map/slice | solution.py:40
  122.3 1.6 slice.602
  124.2 45.4 %fusion.185 = (f32[384]{0:T(512)S(1)}, f32[384,2048]{1,0:T(8,128)S(1)}) fusion(f32[2048]{0:T(1024)S(1)} %get-tuple-element.70, bf16[15,2048]{1,0:T(8,128)(2,1)} %collective-permute-done.1, bf16[384,2048]{1,0:T(8,128)(2,1)} %copy-done.4, f32[2048]{0:T(1024)S(1)} %get-tuple-element.71, f32[2048]{0:T(1024)S(1)} %get-tuple-element.72, ...), kind=kLoop, calls=%fused_computation.397 | loop fusion | flops 143916672 | bytes 5096960 | tf_op jit(solution)/shard_map/reduce_sum | solution.py:67
  170.2 3.9 multiply_reduce_fusion.1
  174.2 20.4 %fusion.75 = (f32[2048]{0:T(1024)}, f32[2048]{0:T(1024)}, f32[2048]{0:T(1024)}, f32[2048]{0:T(1024)}, f32[2048]{0:T(1024)}, /*index=5*/f32[2048]{0:T(1024)}, f32...) fusion(bf16[15,2048]{1,0:T(8,128)(2,1)} %collective-permute-done.1, ...), kind=kLoop, calls=%fused_computation.204 | loop fusion | flops 49526784 | bytes 9586688 | tf_op jit(solution)/shard_map/reduce_sum | solution.py:59
  194.6 4.2 fusion.58
  198.8 15.3 %fusion.74 = (f32[2048]{0:T(1024)S(1)}, f32[2048]{0:T(1024)S(1)}, f32[2048]{0:T(1024)S(1)}, f32[2048]{0:T(1024)S(1)}, f32[2048]{0:T(1024)S(1)}, /*index=5*/f32[2048]{0:T(1024)S(1)}, f32[2048]{0:T(1024)S(1)}) fusion(bf16[384,2048]{1,0:T(8,128)(2,1)S(1)} %get-tuple-element.102, bf16[15,2048]{1,0:T(8,128)(2,1)} %collective-permute-done.1, ...), kind=kLoop, calls=%fused_computation.203 | loop fusion | flops 31442944 | bytes 3264512 | tf_op jit(solution)/shard_map/reduce_sum | solution.py:59
  214.1 7.3 %fusion.59 = (f32[2048]{0:T(1024)S(1)}, f32[2048]{0:T(1024)}, f32[2048]{0:T(1024)}, f32[2048]{0:T(1024)}, f32[2048]{0:T(1024)}, /*index=5*/f32[2048]{0:T(1024)}, f32[2048]{0:T(1024)}, f32[2048]{0:T(1024)}, f32[2048]{0:T(1024)}) fusion(bf16[384,2048]{1,0:T(8,128)(2,1)S(1)} %get-tuple-element.102, bf16[384,2048]{1,0:T(8,128)(2,1)S(1)} %copy-done.5, ...), kind=kLoop, calls=%fused_computation.188 | loop fusion | flops 43235328 | bytes 3280896 | tf_op jit(solution)/shard_map/reduce_sum | solution.py:59
  221.4 3.4 stack.127
  224.8 1.3 copy.101
  226.2 1.7 reshape.259
  228.7 1.7 reshape.273
  230.4 2.9 fusion.160
  233.4 2.1 fusion.189
  235.5 2.6 bitcast_reduce_fusion
  238.2 2.2 fusion.1
  240.4 2.1 fusion.4
  242.5 3.2 fusion.7
  245.7 1.0 fusion.166
  248.0 1.3 reshape.251
  249.3 1.3 pad.4
  250.6 1.3 reshape.252
  251.9 1.5 copy.93
  253.4 1.8 pad_maximum_fusion.5
  255.2 2.0 copy.94
  257.3 1.7 reshape_squeeze.10
  259.0 1.7 reshape_squeeze.11
  260.6 1.5 fusion.190
  262.2 4.6 collective-permute-start.3
  266.7 1.3 collective-permute-start.2
  268.0 3.3 convolution_bitcast_fusion
  271.7 1.5 collective-permute-done.2
  273.5 33.0 %fusion.97 = (bf16[1,384,2048]{2,1,0:T(8,128)(2,1)S(1)}, f32[384,2048]{1,0:T(8,128)S(1)}) fusion(bf16[384,4096]{1,0:T(8,128)(2,1)} %bitcast.138, f32[384]{0:T(512)S(1)} %copy-done.86, f32[2048]{0:T(1024)S(1)} %copy-done.23, bf16[384,2048]{1,0:T(8,128)(2,1)S(1)} %copy-done.8, bf16[15,2048]{1,0:T(8,128)(2,1)} %collective-permute-done.3, ...), kind=kLoop, calls=%fused_computation.236 | loop fusion | flops 148635648 | bytes 8242688 | tf_op jit(solution)/shard_map/concatenate | solution.py:253
  306.5 1.1 fusion.98
  307.7 2.0 pad_maximum_fusion
  309.7 36.1 %reduce-scatter.7.cloned.1.call-done = f32[8,256]{1,0:T(8,128)} async-done(((f32[256,256]{1,0:T(8,128)}), f32[8,256]{1,0:T(8,128)}) %reduce-scatter.7.cloned.1.call-update) | async-done | bytes 8208
  346.6 8.8 %fusion.158 = bf16[2,128,384]{2,1,0:T(8,128)(2,1)} fusion(bf16[3072,2,128]{0,2,1:T(8,128)(2,1)S(1)} %bitcast.142, bf16[384,2,128]{0,2,1:T(8,128)(2,1)S(1)} %bitcast.156, bf16[3072,2,128]{0,2,1:T(8,128)(2,1)S(1)} %bitcast.145, f32[2,3072,384]{2,1,0:T(8,128)} %copy-done.3, f32[2,384]{1,0:T(2,128)S(1)} %copy-done.84, f32[2,384]{1,0:T(2,128)S(1)} %log_add_fusion, ...), kind=kOutput, calls=%fused_computation.319 | convolution fusion | flops 1224572928 | bytes 12985344 | tf_op jit(solution)/shard_map/hqk,khd->qhd/dot_general | solution.py:192
  355.4 1.7 copy.104
  357.2 65.5 %all-gather.10.cloned.1.call-done = bf16[3200,512]{1,0:T(8,128)(2,1)} async-done(((bf16[400,512]{1,0:T(8,128)(2,1)}), bf16[3200,512]{1,0:T(8,128)(2,1)}) %all-gather.10.cloned.1.call-update) | async-done | bytes 3276816 | tf_op jit(solution)/shard_map/all_gather | solution.py:205
  422.7 2.1 slice.604
  424.8 1.9 fusion.188
  426.6 1.8 copy.127
  428.5 2.0 copy.128
  430.5 0.9 slice_bitcast_fusion
  431.7 5.2 fusion.169
  436.9 8.5 %fusion.157 = bf16[2,128,384]{2,1,0:T(8,128)(2,1)S(1)} fusion(bf16[3072,2,128]{0,2,1:T(8,128)(2,1)S(1)} %bitcast.147, f32[2,3072,384]{2,1,0:T(8,128)} %fusion.169, bf16[3072,2,128]{0,2,1:T(8,128)(2,1)S(1)} %bitcast.154, f32[2,3072]{1,0:T(2,128)S(1)} %bitcast.205, f32[2,3072]{1,0:T(2,128)S(1)} %bitcast.203, pred[384]{0:T(512)(128)(4,1)S(1)} %copy-done.88, ...), kind=kOutput, calls=%fused_computation.318 | convolution fusion | flops 1224572928 | bytes 13025664 | tf_op jit(solution)/shard_map/hqk,qhd->khd/dot_general | solution.py:230
  445.4 108.3 %reduce-scatter.5.cloned.1.call-done = f32[128,256]{0,1:T(8,128)} async-done(((f32[4096,256]{0,1:T(8,128)}), f32[128,256]{0,1:T(8,128)}) %reduce-scatter.5.cloned.1.call-update) | async-done | bytes 131088 | tf_op jit(solution)/shard_map/reduce_scatter | solution.py:105
  553.7 1.6 pad_maximum_fusion.8
  555.4 6.5 fusion.163
  563.5 71.1 %all-reduce.3.cloned.1.call-done = f32[136,256]{0,1:T(8,128)} async-done(((f32[136,256]{0,1:T(8,128)}), f32[136,256]{0,1:T(8,128)}) %all-reduce.3.cloned.1.call-update) | async-done | bytes 139280 | tf_op jit(solution)/shard_map/psum | solution.py:113
  634.6 0.9 slice.1359
  636.3 0.9 slice.767
  (233 shorter events, 13.4 us)
Async XLA Ops:
  7.2 223.2 %copy-start = (bf16[1,384,4096]{2,1,0:T(8,128)(2,1)S(1)}, bf16[1,384,4096]{2,1,0:T(8,128)(2,1)}, u32[]{:S(2)}) copy-start(bf16[1,384,4096]{2,1,0:T(8,128)(2,1)} %param.15) | copy-start | bytes 9437188
  7.2 17.7 %copy-start.19 = (bf16[1,384,256]{2,1,0:T(8,128)(2,1)S(1)}, bf16[1,384,256]{2,1,0:T(8,128)(2,1)}, u32[]{:S(2)}) copy-start(bf16[1,384,256]{2,1,0:T(8,128)(2,1)} %param.11) | copy-start | bytes 589828
  7.2 84.8 %all-gather.8.cloned.1.call-start = ((), (), s32[]{:S(2)}) async-start(), calls=%async_computation.5 | async-start | bytes 2297856 | tf_op jit(solution)/shard_map/all_gather | solution.py:91
  10.6 222.8 %all-gather.6.cloned.1.call-start = ((), (), s32[]{:S(2)}) async-start(), calls=%async_computation.2 | async-start | bytes 3538944 | tf_op jit(solution)/shard_map/all_gather | solution.py:159
  11.8 158.3 %copy-start.85 = (f32[384]{0:T(512)}, f32[384]{0:T(512)S(1)}, u32[]{:S(2)}) copy-start(f32[384]{0:T(512)S(1)} %get-tuple-element.106) | copy-start | bytes 4612
  11.8 15.8 %copy-start.18 = (bf16[1,384,256]{2,1,0:T(8,128)(2,1)S(1)}, bf16[1,384,256]{2,1,0:T(8,128)(2,1)}, u32[]{:S(2)}) copy-start(bf16[1,384,256]{2,1,0:T(8,128)(2,1)} %param.10) | copy-start | bytes 589828
  16.7 107.3 %collective-permute-start.1 = (bf16[15,2048]{1,0:T(8,128)(2,1)}, bf16[15,2048]{1,0:T(8,128)(2,1)}, u32[]{:S(2)}, u32[]{:S(2)}) collective-permute-start(bf16[15,2048]{1,0:T(8,128)(2,1)} %get-tuple-element.115), channel_id=1, source_target_pairs={{1,0},{2,1},{3,2},{4,3},{5,4},{6,5},{7,6},{9,8},{10,9},{11,10},{12... | collective-permute-start | bytes 184328 | tf_op jit(solution)/shard_map/ppermute | solution.py:30
  18.0 106.0 %collective-permute-start = (bf16[15,2048]{1,0:T(8,128)(2,1)}, bf16[15,2048]{1,0:T(8,128)(2,1)}, u32[]{:S(2)}, u32[]{:S(2)}) collective-permute-start(bf16[15,2048]{1,0:T(8,128)(2,1)} %get-tuple-element.114), channel_id=1, source_target_pairs={{0,1},{1,2},{2,3},{3,4},{4,5},{5,6},{6,7},{8,9},{9,10},{10,11},{11... | collective-permute-start | bytes 184328 | tf_op jit(solution)/shard_map/ppermute | solution.py:28
  27.6 318.2 %reduce-scatter.7.cloned.1.call-start = ((), (), s32[]{:S(2)}) async-start(), calls=%async_computation.7 | async-start | bytes 270336
  95.2 19.6 %copy-start.2 = (f32[2048,31]{1,0:T(8,128)S(1)}, f32[2048,31]{1,0:T(8,128)}, u32[]{:S(2)}) copy-start(f32[2048,31]{1,0:T(8,128)} %reshape.264) | copy-start | bytes 761860
  114.8 9.2 %copy-start.22 = (f32[2048]{0:T(1024)}, f32[2048]{0:T(1024)S(1)}, u32[]{:S(2)}) copy-start(f32[2048]{0:T(1024)S(1)} %get-tuple-element.70) | copy-start | bytes 24580
  114.8 9.2 %copy-start.24 = (f32[2048]{0:T(1024)}, f32[2048]{0:T(1024)S(1)}, u32[]{:S(2)}) copy-start(f32[2048]{0:T(1024)S(1)} %get-tuple-element.71) | copy-start | bytes 24580
  114.8 9.2 %copy-start.26 = (f32[2048]{0:T(1024)}, f32[2048]{0:T(1024)S(1)}, u32[]{:S(2)}) copy-start(f32[2048]{0:T(1024)S(1)} %get-tuple-element.72) | copy-start | bytes 24580
  114.8 9.2 %copy-start.28 = (f32[2048]{0:T(1024)}, f32[2048]{0:T(1024)S(1)}, u32[]{:S(2)}) copy-start(f32[2048]{0:T(1024)S(1)} %get-tuple-element.73) | copy-start | bytes 24580
  114.8 9.2 %copy-start.30 = (f32[2048]{0:T(1024)}, f32[2048]{0:T(1024)S(1)}, u32[]{:S(2)}) copy-start(f32[2048]{0:T(1024)S(1)} %get-tuple-element.74) | copy-start | bytes 24580
  114.8 9.2 %copy-start.32 = (f32[2048]{0:T(1024)}, f32[2048]{0:T(1024)S(1)}, u32[]{:S(2)}) copy-start(f32[2048]{0:T(1024)S(1)} %get-tuple-element.75) | copy-start | bytes 24580
  114.8 9.2 %copy-start.34 = (f32[2048]{0:T(1024)}, f32[2048]{0:T(1024)S(1)}, u32[]{:S(2)}) copy-start(f32[2048]{0:T(1024)S(1)} %get-tuple-element.76) | copy-start | bytes 24580
  114.8 9.2 %copy-start.36 = (f32[2048]{0:T(1024)}, f32[2048]{0:T(1024)S(1)}, u32[]{:S(2)}) copy-start(f32[2048]{0:T(1024)S(1)} %get-tuple-element.77) | copy-start | bytes 24580
  114.8 9.2 %copy-start.38 = (f32[2048]{0:T(1024)}, f32[2048]{0:T(1024)S(1)}, u32[]{:S(2)}) copy-start(f32[2048]{0:T(1024)S(1)} %get-tuple-element.78) | copy-start | bytes 24580
  114.8 9.2 %copy-start.40 = (f32[2048]{0:T(1024)}, f32[2048]{0:T(1024)S(1)}, u32[]{:S(2)}) copy-start(f32[2048]{0:T(1024)S(1)} %get-tuple-element.79) | copy-start | bytes 24580
  114.9 9.2 %copy-start.42 = (f32[2048]{0:T(1024)}, f32[2048]{0:T(1024)S(1)}, u32[]{:S(2)}) copy-start(f32[2048]{0:T(1024)S(1)} %get-tuple-element.80) | copy-start | bytes 24580
  114.9 9.2 %copy-start.44 = (f32[2048]{0:T(1024)}, f32[2048]{0:T(1024)S(1)}, u32[]{:S(2)}) copy-start(f32[2048]{0:T(1024)S(1)} %get-tuple-element.81) | copy-start | bytes 24580
  114.9 9.2 %copy-start.46 = (f32[2048]{0:T(1024)}, f32[2048]{0:T(1024)S(1)}, u32[]{:S(2)}) copy-start(f32[2048]{0:T(1024)S(1)} %get-tuple-element.82) | copy-start | bytes 24580
  114.9 9.2 %copy-start.48 = (f32[2048]{0:T(1024)}, f32[2048]{0:T(1024)S(1)}, u32[]{:S(2)}) copy-start(f32[2048]{0:T(1024)S(1)} %get-tuple-element.83) | copy-start | bytes 24580
  114.9 9.2 %copy-start.50 = (f32[2048]{0:T(1024)}, f32[2048]{0:T(1024)S(1)}, u32[]{:S(2)}) copy-start(f32[2048]{0:T(1024)S(1)} %get-tuple-element.84) | copy-start | bytes 24580
  114.9 9.2 %copy-start.52 = (f32[2048]{0:T(1024)}, f32[2048]{0:T(1024)S(1)}, u32[]{:S(2)}) copy-start(f32[2048]{0:T(1024)S(1)} %get-tuple-element.85) | copy-start | bytes 24580
  114.9 9.2 %copy-start.54 = (f32[2048]{0:T(1024)}, f32[2048]{0:T(1024)S(1)}, u32[]{:S(2)}) copy-start(f32[2048]{0:T(1024)S(1)} %get-tuple-element.86) | copy-start | bytes 24580
  114.9 9.2 %copy-start.56 = (f32[2048]{0:T(1024)}, f32[2048]{0:T(1024)S(1)}, u32[]{:S(2)}) copy-start(f32[2048]{0:T(1024)S(1)} %get-tuple-element.87) | copy-start | bytes 24580
  114.9 7.4 %copy-start.15 = (bf16[4352,256]{1,0:T(8,128)(2,1)S(1)}, bf16[4352,256]{1,0:T(8,128)(2,1)}, u32[]{:S(2)}) copy-start(bf16[4352,256]{1,0:T(8,128)(2,1)} %all-gather.8.cloned.1.call-done) | copy-start | bytes 6684676
  121.5 48.1 %copy-start.58 = (f32[2048]{0:T(1024)}, f32[2048]{0:T(1024)S(1)}, u32[]{:S(2)}) copy-start(f32[2048]{0:T(1024)S(1)} %get-tuple-element.88) | copy-start | bytes 24580
  121.5 48.1 %copy-start.60 = (f32[2048]{0:T(1024)}, f32[2048]{0:T(1024)S(1)}, u32[]{:S(2)}) copy-start(f32[2048]{0:T(1024)S(1)} %get-tuple-element.89) | copy-start | bytes 24580
  121.5 48.1 %copy-start.62 = (f32[2048]{0:T(1024)}, f32[2048]{0:T(1024)S(1)}, u32[]{:S(2)}) copy-start(f32[2048]{0:T(1024)S(1)} %get-tuple-element.90) | copy-start | bytes 24580
  121.5 48.1 %copy-start.64 = (f32[2048]{0:T(1024)}, f32[2048]{0:T(1024)S(1)}, u32[]{:S(2)}) copy-start(f32[2048]{0:T(1024)S(1)} %get-tuple-element.91) | copy-start | bytes 24580
  121.6 48.1 %copy-start.66 = (f32[2048]{0:T(1024)}, f32[2048]{0:T(1024)S(1)}, u32[]{:S(2)}) copy-start(f32[2048]{0:T(1024)S(1)} %get-tuple-element.92) | copy-start | bytes 24580
  121.6 48.1 %copy-start.68 = (f32[2048]{0:T(1024)}, f32[2048]{0:T(1024)S(1)}, u32[]{:S(2)}) copy-start(f32[2048]{0:T(1024)S(1)} %get-tuple-element.93) | copy-start | bytes 24580
  121.6 48.1 %copy-start.70 = (f32[2048]{0:T(1024)}, f32[2048]{0:T(1024)S(1)}, u32[]{:S(2)}) copy-start(f32[2048]{0:T(1024)S(1)} %get-tuple-element.94) | copy-start | bytes 24580
  121.6 48.1 %copy-start.72 = (f32[2048]{0:T(1024)}, f32[2048]{0:T(1024)S(1)}, u32[]{:S(2)}) copy-start(f32[2048]{0:T(1024)S(1)} %get-tuple-element.95) | copy-start | bytes 24580
  121.6 48.1 %copy-start.74 = (f32[2048]{0:T(1024)}, f32[2048]{0:T(1024)S(1)}, u32[]{:S(2)}) copy-start(f32[2048]{0:T(1024)S(1)} %get-tuple-element.96) | copy-start | bytes 24580
  121.6 48.1 %copy-start.76 = (f32[2048]{0:T(1024)}, f32[2048]{0:T(1024)S(1)}, u32[]{:S(2)}) copy-start(f32[2048]{0:T(1024)S(1)} %get-tuple-element.97) | copy-start | bytes 24580
  121.6 48.1 %copy-start.78 = (f32[2048]{0:T(1024)}, f32[2048]{0:T(1024)S(1)}, u32[]{:S(2)}) copy-start(f32[2048]{0:T(1024)S(1)} %get-tuple-element.98) | copy-start | bytes 24580
  121.6 48.1 %copy-start.80 = (f32[2048]{0:T(1024)}, f32[2048]{0:T(1024)S(1)}, u32[]{:S(2)}) copy-start(f32[2048]{0:T(1024)S(1)} %get-tuple-element.99) | copy-start | bytes 24580
  124.2 46.0 %copy-start.16 = (bf16[1,384,2048]{2,1,0:T(8,128)(2,1)S(1)}, bf16[1,384,2048]{2,1,0:T(8,128)(2,1)}, u32[]{:S(2)}) copy-start(bf16[1,384,2048]{2,1,0:T(8,128)(2,1)} %param.19) | copy-start | bytes 4718596
  169.7 4.4 copy-start.6
  174.2 20.4 %copy-start.5 = (bf16[384,2048]{1,0:T(8,128)(2,1)S(1)}, bf16[384,2048]{1,0:T(8,128)(2,1)}, u32[]{:S(2)}) copy-start(bf16[384,2048]{1,0:T(8,128)(2,1)} %copy-done.4) | copy-start | bytes 4718596
  194.6 19.5 %copy-start.7 = (bf16[384,2048]{1,0:T(8,128)(2,1)}, bf16[384,2048]{1,0:T(8,128)(2,1)S(1)}, u32[]{:S(2)}) copy-start(bf16[384,2048]{1,0:T(8,128)(2,1)S(1)} %get-tuple-element.102) | copy-start | bytes 4718596
  233.3 2.2 copy-start.20
  233.3 189.4 %all-gather.10.cloned.1.call-start = ((), (), s32[]{:S(2)}) async-start(), calls=%async_computation.6 | async-start | bytes 3686400 | tf_op jit(solution)/shard_map/all_gather | solution.py:205
  235.5 2.6 copy-start.10
  235.5 10.2 %copy-start.13 = (bf16[3072,256]{0,1:T(8,128)(2,1)}, bf16[3072,256]{0,1:T(8,128)(2,1)S(1)}, u32[]{:S(2)}) copy-start(bf16[3072,256]{0,1:T(8,128)(2,1)S(1)} %get-tuple-element.110) | copy-start | bytes 4718596
  238.2 4.4 copy-start.3
  257.2 296.5 %reduce-scatter.5.cloned.1.call-start = ((), (), s32[]{:S(2)}) async-start(), calls=%async_computation.3 | async-start | bytes 4325376 | tf_op jit(solution)/shard_map/reduce_scatter | solution.py:105
  262.2 9.6 %collective-permute-start.3 = (bf16[15,2048]{1,0:T(8,128)(2,1)}, bf16[15,2048]{1,0:T(8,128)(2,1)}, u32[]{:S(2)}, u32[]{:S(2)}) collective-permute-start(bf16[15,2048]{1,0:T(8,128)(2,1)} %get-tuple-element.113), channel_id=1, source_target_pairs={{0,1},{1,2},{2,3},{3,4},{4,5},{5,6},{6,7},{8,9},{9,10},{10,11},{11... | collective-permute-start | bytes 184328 | tf_op jit(solution)/shard_map/ppermute | solution.py:28
  266.7 6.5 %collective-permute-start.2 = (bf16[15,2048]{1,0:T(8,128)(2,1)}, bf16[15,2048]{1,0:T(8,128)(2,1)}, u32[]{:S(2)}, u32[]{:S(2)}) collective-permute-start(bf16[15,2048]{1,0:T(8,128)(2,1)} %get-tuple-element.112), channel_id=1, source_target_pairs={{1,0},{2,1},{3,2},{4,3},{5,4},{6,5},{7,6},{9,8},{10,9},{11,10},{12... | collective-permute-start | bytes 184328 | tf_op jit(solution)/shard_map/ppermute | solution.py:30
  271.7 362.9 %all-reduce.3.cloned.1.call-start = ((), (), s32[]{:S(2)}) async-start(), calls=%async_computation.4 | async-start | bytes 524288 | tf_op jit(solution)/shard_map/psum | solution.py:113
  271.7 34.8 %copy-start.9 = (bf16[1,384,4096]{2,1,0:T(8,128)(2,1)S(1)}, bf16[1,384,4096]{2,1,0:T(8,128)(2,1)}, u32[]{:S(2)}) copy-start(bf16[1,384,4096]{2,1,0:T(8,128)(2,1)} %param.16) | copy-start | bytes 9437188
  307.6 39.0 %copy-start.11 = (bf16[3072,256]{0,1:T(8,128)(2,1)S(1)}, bf16[3072,256]{0,1:T(8,128)(2,1)}, u32[]{:S(2)}) copy-start(bf16[3072,256]{0,1:T(8,128)(2,1)} %copy-done.10) | copy-start | bytes 4718596
  307.7 39.0 %copy-start.14 = (bf16[3072,256]{0,1:T(8,128)(2,1)S(1)}, bf16[3072,256]{0,1:T(8,128)(2,1)}, u32[]{:S(2)}) copy-start(bf16[3072,256]{0,1:T(8,128)(2,1)} %copy-done.13) | copy-start | bytes 4718596
  307.7 39.0 %copy-start.84 = (f32[2,384]{1,0:T(2,128)S(1)}, f32[2,384]{1,0:T(2,128)}, u32[]{:S(2)}) copy-start(f32[2,384]{1,0:T(2,128)} %copy-done.83) | copy-start | bytes 9220
  426.6 1.9 copy-start.12
  426.6 5.0 copy-start.21
  431.6 5.2 copy-start.87
  431.6 5.2 copy-start.17
  431.7 5.2 copy-start.88
  555.4 83.3 %copy-start.1 = (bf16[1,384,4096]{2,1,0:T(8,128)(2,1)S(1)}, bf16[1,384,4096]{2,1,0:T(8,128)(2,1)}, u32[]{:S(2)}) copy-start(bf16[1,384,4096]{2,1,0:T(8,128)(2,1)} %param.15) | copy-start | bytes 9437188
  (35 other events, 62.9 us)
Sparse Core Ops, SparseCore 0:
  11.3 80.6 all-gather.7
  93.8 73.0 all-gather.5
  233.4 112.3 reduce-scatter.6
  347.4 75.2 all-gather.9
  426.7 126.9 reduce-scatter.4
  556.2 78.3 all-reduce.2
where the time goes:
time: 658 us; the launch traced here: 646 us
  waiting for transfers between devices  345 us (52%)
  other arithmetic  151 us (23%)
  local copies, waits for them, and re-layouts  78.7 us (12%)
  matrix products  42 us (6%)
  between operations  16.7 us (3%)
  starting transfers between devices  12.6 us (2%)
    reduce_scatter x1, waiting for transfers between devices, reduce_grads(): lax.psum_scatter(proj_term, 'dp', scatter_dimension=0, tiled=True)  108 us
    psum x1, waiting for transfers between devices, reduce_grads(): total = lax.psum(jnp.concatenate([proj_part, tail_part], axis=0), 'tm')  71.1 us
    all_gather x1, waiting for transfers between devices, per_device(): query_grad = lax.all_gather(packed_rows, 'tm', axis=0, tiled=False)  65.5 us
    all_gather x1, waiting for transfers between devices, gather_params(): full = lax.all_gather(block, 'dp', axis=0, tiled=False)  62.8 us
    reduce_sum x4, other arithmetic, tap_products(): jnp.sum(grad_f * padded[tap:tap + frame_rows].astype(jnp.float32), axis=0)  47.2 us
    reduce_sum x1, other arithmetic, norm_backward(): centre = mixed - jnp.mean(mixed, axis=-1, keepdims=True)  45.4 us
    unnamed x7, waiting for transfers between devices  36.2 us
    concatenate x3, other arithmetic, per_device(): jnp.concatenate([first_half, second_half], axis=-1).astype(jnp.bfloat16)  36.1 us
  transfers between devices with their start and end apart: 10, of which 6 were waited for; matrix products, arithmetic and copies ran while one was open for 40% of the time, Pallas kernels for 0%

commit v1 on v0

--- a/solution.py
+++ b/solution.py
@@ -110,7 +110,12 @@
     tail_rows = -(-tail_cols // width)
     tail = jnp.pad(tail, ((0, 0), (0, tail_rows * width - tail_cols))).reshape(-1, width)
     tail_part = lax.psum_scatter(tail, "dp", scatter_dimension=0, tiled=True)
-    total = lax.psum(jnp.concatenate([proj_part, tail_part], axis=0), "tm")
+
+    def wait_flows_over_axis(obj, row_axis):
+        finding = lax.all_gather(obj, axis_name=row_axis)
+        return jnp.sum(finding, axis=0)
+
+    total = wait_flows_over_axis(jnp.concatenate([proj_part, tail_part], axis=0), "tm")
     proj_rows = proj_part.shape[0]
     proj_total = total[:proj_rows]
     flat_tail = total[proj_rows:].reshape(-1)

time: 658 us -> 620 us (0.942)
  waiting for transfers between devices: 345 us -> 307 us
    psum x1 -> x0, waiting for transfers between devices: 71.1 us -> none  [reduce_grads(): total = lax.psum(jnp.concatenate([proj_part, tail_part], axis=0), 'tm')]
    all_gather x0 -> x1, waiting for transfers between devices: none -> 24.6 us  [wait_flows_over_axis(): finding = lax.all_gather(obj, axis_name=row_axis)]
    reduce_scatter x1, waiting for transfers between devices: 108 us -> 116 us  [reduce_grads(): lax.psum_scatter(proj_term, 'dp', scatter_dimension=0, tiled=True)]
    unnamed x197 -> x195, local copies, waits for them, and re-layouts: 17 us -> 17.1 us
  transfers between devices with their start and end apart: 10 -> 10, of which waited for: 6 -> 6; matrix products, arithmetic and copies ran while one was open for 40% -> 43% of each run, Pallas kernels for 0% -> 0%
where the time goes in v1:
time: 620 us; the launch traced here: 608 us
  waiting for transfers between devices  307 us (50%)
  other arithmetic  152 us (25%)
  local copies, waits for them, and re-layouts  78.2 us (13%)
  matrix products  41.8 us (7%)
  between operations  16.7 us (3%)
  starting transfers between devices  12.6 us (2%)
    reduce_scatter x1, waiting for transfers between devices, reduce_grads(): lax.psum_scatter(proj_term, 'dp', scatter_dimension=0, tiled=True)  116 us
    all_gather x1, waiting for transfers between devices, per_device(): query_grad = lax.all_gather(packed_rows, 'tm', axis=0, tiled=False)  65.5 us
    all_gather x1, waiting for transfers between devices, gather_params(): full = lax.all_gather(block, 'dp', axis=0, tiled=False)  62.8 us
    reduce_sum x4, other arithmetic, tap_products(): jnp.sum(grad_f * padded[tap:tap + frame_rows].astype(jnp.float32), axis=0)  47.2 us
    reduce_sum x1, other arithmetic, norm_backward(): centre = mixed - jnp.mean(mixed, axis=-1, keepdims=True)  45.4 us
    unnamed x7, waiting for transfers between devices  36.2 us
    concatenate x3, other arithmetic, per_device(): jnp.concatenate([first_half, second_half], axis=-1).astype(jnp.bfloat16)  36.1 us
    slice x2, local copies, waits for them, and re-layouts, depthwise(): kernel_f[:, tap]  26.1 us
  transfers between devices with their start and end apart: 10, of which 6 were waited for; matrix products, arithmetic and copies ran while one was open for 43% of the time, Pallas kernels for 0%

profile of v1, /device:TPU:4, one launch (start us, length us, event | category | flops | bytes accessed | tf_op | source)
XLA Modules:
  0.0 608.0 jit_solution(5456365903199159374)
XLA Ops:
  7.2 1.0 copy.82
  9.1 1.5 pad_maximum_fusion.9
  11.8 2.9 fusion.11
  14.8 1.2 copy-done.4
  16.7 1.3 collective-permute-start.1
  18.0 5.2 collective-permute-start
  23.2 1.7 copy.79
  25.7 1.8 pad_maximum_fusion.6
  29.2 62.8 %all-gather.10.cloned.1.call-done = bf16[4352,256]{1,0:T(8,128)(2,1)} async-done(((bf16[136,256]{1,0:T(8,128)(2,1)}), bf16[4352,256]{1,0:T(8,128)(2,1)}) %all-gather.10.cloned.1.call-update) | async-done | bytes 2228240 | tf_op jit(solution)/shard_map/all_gather | solution.py:91
  92.0 0.9 slice.619
  92.9 2.2 reshape.264
  95.2 19.6 %slice_reduce_fusion.30 = (f32[2048]{0:T(1024)S(1)}, f32[2048]{0:T(1024)S(1)}, f32[2048]{0:T(1024)S(1)}, f32[2048]{0:T(1024)S(1)}, f32[2048]{0:T(1024)S(1)}, /*i...) fusion(f32[2048,31]{1,0:T(8,128)} %reshape.264), kind=kLoop, calls=%fused_computation.353 | loop fusion | bytes 311296 | tf_op jit(solution)/shard_map/slice | solution.py:40
  114.9 6.6 %slice_reduce_fusion.29 = (f32[2048]{0:T(1024)S(1)}, f32[2048]{0:T(1024)S(1)}, f32[2048]{0:T(1024)S(1)}, f32[2048]{0:T(1024)S(1)}, f32[2048]{0:T(1024)S(1)}, /*i...) fusion(f32[2048,31]{1,0:T(8,128)S(1)} %copy-done.2), kind=kLoop, calls=%fused_computation.352 | loop fusion | bytes 196608 | tf_op jit(solution)/shard_map/slice | solution.py:40
  122.3 1.6 slice.602
  124.2 45.4 %fusion.185 = (f32[384]{0:T(512)S(1)}, f32[384,2048]{1,0:T(8,128)S(1)}) fusion(f32[2048]{0:T(1024)S(1)} %get-tuple-element.70, bf16[15,2048]{1,0:T(8,128)(2,1)} %collective-permute-done.1, bf16[384,2048]{1,0:T(8,128)(2,1)} %copy-done.4, f32[2048]{0:T(1024)S(1)} %get-tuple-element.71, f32[2048]{0:T(1024)S(1)} %get-tuple-element.72, ...), kind=kLoop, calls=%fused_computation.398 | loop fusion | flops 143916672 | bytes 5096960 | tf_op jit(solution)/shard_map/reduce_sum | solution.py:67
  170.2 3.9 multiply_reduce_fusion.1
  174.2 20.4 %fusion.75 = (f32[2048]{0:T(1024)}, f32[2048]{0:T(1024)}, f32[2048]{0:T(1024)}, f32[2048]{0:T(1024)}, f32[2048]{0:T(1024)}, /*index=5*/f32[2048]{0:T(1024)}, f32...) fusion(bf16[15,2048]{1,0:T(8,128)(2,1)} %collective-permute-done.1, ...), kind=kLoop, calls=%fused_computation.204 | loop fusion | flops 49526784 | bytes 9586688 | tf_op jit(solution)/shard_map/reduce_sum | solution.py:59
  194.6 4.2 fusion.58
  198.8 15.3 %fusion.74 = (f32[2048]{0:T(1024)S(1)}, f32[2048]{0:T(1024)S(1)}, f32[2048]{0:T(1024)S(1)}, f32[2048]{0:T(1024)S(1)}, f32[2048]{0:T(1024)S(1)}, /*index=5*/f32[2048]{0:T(1024)S(1)}, f32[2048]{0:T(1024)S(1)}) fusion(bf16[384,2048]{1,0:T(8,128)(2,1)S(1)} %get-tuple-element.102, bf16[15,2048]{1,0:T(8,128)(2,1)} %collective-permute-done.1, ...), kind=kLoop, calls=%fused_computation.203 | loop fusion | flops 31442944 | bytes 3264512 | tf_op jit(solution)/shard_map/reduce_sum | solution.py:59
  214.1 7.3 %fusion.59 = (f32[2048]{0:T(1024)S(1)}, f32[2048]{0:T(1024)}, f32[2048]{0:T(1024)}, f32[2048]{0:T(1024)}, f32[2048]{0:T(1024)}, /*index=5*/f32[2048]{0:T(1024)}, f32[2048]{0:T(1024)}, f32[2048]{0:T(1024)}, f32[2048]{0:T(1024)}) fusion(bf16[384,2048]{1,0:T(8,128)(2,1)S(1)} %get-tuple-element.102, bf16[384,2048]{1,0:T(8,128)(2,1)S(1)} %copy-done.5, ...), kind=kLoop, calls=%fused_computation.188 | loop fusion | flops 43235328 | bytes 3280896 | tf_op jit(solution)/shard_map/reduce_sum | solution.py:59
  221.4 3.4 stack.127
  224.8 1.3 copy.98
  226.2 1.7 reshape.259
  228.7 1.7 reshape.274
  230.4 2.9 fusion.160
  233.4 2.1 fusion.189
  235.5 2.6 bitcast_reduce_fusion
  238.2 2.2 fusion.1
  240.4 2.1 fusion.4
  242.5 3.2 fusion.7
  245.7 1.0 fusion.166
  248.0 1.3 reshape.251
  249.3 1.3 pad.4
  250.6 1.3 reshape.252
  251.9 1.5 copy.90
  253.4 1.8 pad_maximum_fusion.5
  255.2 2.0 copy.91
  257.3 1.7 reshape_squeeze.10
  259.0 1.7 reshape_squeeze.11
  260.6 1.5 fusion.190
  262.2 4.6 collective-permute-start.3
  266.7 1.3 collective-permute-start.2
  268.0 3.3 convolution_bitcast_fusion
  271.7 1.5 collective-permute-done.2
  273.5 33.0 %fusion.97 = (bf16[1,384,2048]{2,1,0:T(8,128)(2,1)S(1)}, f32[384,2048]{1,0:T(8,128)S(1)}) fusion(bf16[384,4096]{1,0:T(8,128)(2,1)} %bitcast.140, f32[384]{0:T(512)S(1)} %copy-done.86, f32[2048]{0:T(1024)S(1)} %copy-done.23, bf16[384,2048]{1,0:T(8,128)(2,1)S(1)} %copy-done.8, bf16[15,2048]{1,0:T(8,128)(2,1)} %collective-permute-done.3, ...), kind=kLoop, calls=%fused_computation.236 | loop fusion | flops 148635648 | bytes 8242688 | tf_op jit(solution)/shard_map/concatenate | solution.py:258
  306.5 1.1 fusion.98
  307.7 2.0 pad_maximum_fusion
  309.7 36.1 %reduce-scatter.7.cloned.1.call-done = f32[8,256]{1,0:T(8,128)} async-done(((f32[256,256]{1,0:T(8,128)}), f32[8,256]{1,0:T(8,128)}) %reduce-scatter.7.cloned.1.call-update) | async-done | bytes 8208
  346.6 8.8 %fusion.158 = bf16[2,128,384]{2,1,0:T(8,128)(2,1)} fusion(bf16[3072,2,128]{0,2,1:T(8,128)(2,1)S(1)} %bitcast.144, bf16[384,2,128]{0,2,1:T(8,128)(2,1)S(1)} %bitcast.159, bf16[3072,2,128]{0,2,1:T(8,128)(2,1)S(1)} %bitcast.147, f32[2,3072,384]{2,1,0:T(8,128)} %copy-done.3, f32[2,384]{1,0:T(2,128)S(1)} %copy-done.84, f32[2,384]{1,0:T(2,128)S(1)} %log_add_fusion, ...), kind=kOutput, calls=%fused_computation.319 | convolution fusion | flops 1224572928 | bytes 12985344 | tf_op jit(solution)/shard_map/hqk,khd->qhd/dot_general | solution.py:197
  355.4 1.7 copy.101
  357.2 65.5 %all-gather.12.cloned.1.call-done = bf16[3200,512]{1,0:T(8,128)(2,1)} async-done(((bf16[400,512]{1,0:T(8,128)(2,1)}), bf16[3200,512]{1,0:T(8,128)(2,1)}) %all-gather.12.cloned.1.call-update) | async-done | bytes 3276816 | tf_op jit(solution)/shard_map/all_gather | solution.py:210
  422.7 2.1 slice.604
  424.8 1.9 fusion.188
  426.6 1.8 copy.123
  428.5 2.0 copy.124
  430.5 0.9 slice_bitcast_fusion
  432.2 5.2 fusion.169
  437.4 116.3 %reduce-scatter.5.cloned.1.call-done = f32[128,256]{0,1:T(8,128)} async-done(((f32[4096,256]{0,1:T(8,128)}), f32[128,256]{0,1:T(8,128)}) %reduce-scatter.5.cloned.1.call-update) | async-done | bytes 131088 | tf_op jit(solution)/shard_map/reduce_scatter | solution.py:105
  553.7 0.9 pad_maximum_fusion.8
  556.2 8.3 %fusion.157 = bf16[2,128,384]{2,1,0:T(8,128)(2,1)S(1)} fusion(bf16[3072,2,128]{0,2,1:T(8,128)(2,1)S(1)} %bitcast.149, f32[2,3072,384]{2,1,0:T(8,128)} %fusion.169, bf16[3072,2,128]{0,2,1:T(8,128)(2,1)S(1)} %bitcast.156, f32[2,3072]{1,0:T(2,128)S(1)} %bitcast.207, f32[2,3072]{1,0:T(2,128)S(1)} %bitcast.205, pred[384]{0:T(512)(128)(4,1)S(1)} %copy-done.87, ...), kind=kOutput, calls=%fused_computation.318 | convolution fusion | flops 1224572928 | bytes 13025664 | tf_op jit(solution)/shard_map/hqk,qhd->khd/dot_general | solution.py:235
  565.4 6.5 %fusion.163 = bf16[2,128,384]{2,1,0:T(8,128)(2,1)S(1)} fusion(bf16[3072,2,128]{0,2,1:T(8,128)(2,1)} %bitcast.155, f32[2,3072,384]{2,1,0:T(8,128)} %fusion.169, f32[2,3072]{1,0:T(2,128)S(1)} %bitcast.206, pred[384]{0:T(512)(128)(4,1)S(1)} %copy-done.87), kind=kOutput, calls=%fused_computation.322 | convolution fusion | flops 613515264 | bytes 11231616 | tf_op jit(solution)/shard_map/hqk,qhd->khd/dot_general | solution.py:226
  571.9 0.8 copy.103
  572.7 24.6 %all-gather.14.cloned.1.call-done = f32[1088,256]{1,0:T(8,128)} async-done(((f32[136,256]{1,0:T(8,128)}), f32[1088,256]{1,0:T(8,128)}) %all-gather.14.cloned.1.call-update) | async-done | bytes 1114128 | tf_op jit(solution)/shard_map/all_gather | solution.py:115
  597.3 1.3 reduce_sum.379
  (231 shorter events, 14.5 us)
Async XLA Ops:
  7.2 223.2 %copy-start = (bf16[1,384,4096]{2,1,0:T(8,128)(2,1)S(1)}, bf16[1,384,4096]{2,1,0:T(8,128)(2,1)}, u32[]{:S(2)}) copy-start(bf16[1,384,4096]{2,1,0:T(8,128)(2,1)} %param.15) | copy-start | bytes 9437188
  7.2 17.7 %copy-start.19 = (bf16[1,384,256]{2,1,0:T(8,128)(2,1)S(1)}, bf16[1,384,256]{2,1,0:T(8,128)(2,1)}, u32[]{:S(2)}) copy-start(bf16[1,384,256]{2,1,0:T(8,128)(2,1)} %param.11) | copy-start | bytes 589828
  7.2 84.8 %all-gather.10.cloned.1.call-start = ((), (), s32[]{:S(2)}) async-start(), calls=%async_computation.4 | async-start | bytes 2297856 | tf_op jit(solution)/shard_map/all_gather | solution.py:91
  10.6 222.8 %all-gather.8.cloned.1.call-start = ((), (), s32[]{:S(2)}) async-start(), calls=%async_computation.2 | async-start | bytes 3538944 | tf_op jit(solution)/shard_map/all_gather | solution.py:164
  11.8 158.3 %copy-start.85 = (f32[384]{0:T(512)}, f32[384]{0:T(512)S(1)}, u32[]{:S(2)}) copy-start(f32[384]{0:T(512)S(1)} %get-tuple-element.106) | copy-start | bytes 4612
  11.8 15.8 %copy-start.18 = (bf16[1,384,256]{2,1,0:T(8,128)(2,1)S(1)}, bf16[1,384,256]{2,1,0:T(8,128)(2,1)}, u32[]{:S(2)}) copy-start(bf16[1,384,256]{2,1,0:T(8,128)(2,1)} %param.10) | copy-start | bytes 589828
  16.7 107.3 %collective-permute-start.1 = (bf16[15,2048]{1,0:T(8,128)(2,1)}, bf16[15,2048]{1,0:T(8,128)(2,1)}, u32[]{:S(2)}, u32[]{:S(2)}) collective-permute-start(bf16[15,2048]{1,0:T(8,128)(2,1)} %get-tuple-element.115), channel_id=1, source_target_pairs={{1,0},{2,1},{3,2},{4,3},{5,4},{6,5},{7,6},{9,8},{10,9},{11,10},{12... | collective-permute-start | bytes 184328 | tf_op jit(solution)/shard_map/ppermute | solution.py:30
  18.0 106.0 %collective-permute-start = (bf16[15,2048]{1,0:T(8,128)(2,1)}, bf16[15,2048]{1,0:T(8,128)(2,1)}, u32[]{:S(2)}, u32[]{:S(2)}) collective-permute-start(bf16[15,2048]{1,0:T(8,128)(2,1)} %get-tuple-element.114), channel_id=1, source_target_pairs={{0,1},{1,2},{2,3},{3,4},{4,5},{5,6},{6,7},{8,9},{9,10},{10,11},{11... | collective-permute-start | bytes 184328 | tf_op jit(solution)/shard_map/ppermute | solution.py:28
  27.6 318.2 %reduce-scatter.7.cloned.1.call-start = ((), (), s32[]{:S(2)}) async-start(), calls=%async_computation.7 | async-start | bytes 270336
  95.2 19.6 %copy-start.2 = (f32[2048,31]{1,0:T(8,128)S(1)}, f32[2048,31]{1,0:T(8,128)}, u32[]{:S(2)}) copy-start(f32[2048,31]{1,0:T(8,128)} %reshape.264) | copy-start | bytes 761860
  114.8 9.2 %copy-start.22 = (f32[2048]{0:T(1024)}, f32[2048]{0:T(1024)S(1)}, u32[]{:S(2)}) copy-start(f32[2048]{0:T(1024)S(1)} %get-tuple-element.70) | copy-start | bytes 24580
  114.8 9.2 %copy-start.24 = (f32[2048]{0:T(1024)}, f32[2048]{0:T(1024)S(1)}, u32[]{:S(2)}) copy-start(f32[2048]{0:T(1024)S(1)} %get-tuple-element.71) | copy-start | bytes 24580
  114.8 9.2 %copy-start.26 = (f32[2048]{0:T(1024)}, f32[2048]{0:T(1024)S(1)}, u32[]{:S(2)}) copy-start(f32[2048]{0:T(1024)S(1)} %get-tuple-element.72) | copy-start | bytes 24580
  114.8 9.2 %copy-start.28 = (f32[2048]{0:T(1024)}, f32[2048]{0:T(1024)S(1)}, u32[]{:S(2)}) copy-start(f32[2048]{0:T(1024)S(1)} %get-tuple-element.73) | copy-start | bytes 24580
  114.8 9.2 %copy-start.30 = (f32[2048]{0:T(1024)}, f32[2048]{0:T(1024)S(1)}, u32[]{:S(2)}) copy-start(f32[2048]{0:T(1024)S(1)} %get-tuple-element.74) | copy-start | bytes 24580
  114.8 9.2 %copy-start.32 = (f32[2048]{0:T(1024)}, f32[2048]{0:T(1024)S(1)}, u32[]{:S(2)}) copy-start(f32[2048]{0:T(1024)S(1)} %get-tuple-element.75) | copy-start | bytes 24580
  114.8 9.2 %copy-start.34 = (f32[2048]{0:T(1024)}, f32[2048]{0:T(1024)S(1)}, u32[]{:S(2)}) copy-start(f32[2048]{0:T(1024)S(1)} %get-tuple-element.76) | copy-start | bytes 24580
  114.8 9.2 %copy-start.36 = (f32[2048]{0:T(1024)}, f32[2048]{0:T(1024)S(1)}, u32[]{:S(2)}) copy-start(f32[2048]{0:T(1024)S(1)} %get-tuple-element.77) | copy-start | bytes 24580
  114.8 9.2 %copy-start.38 = (f32[2048]{0:T(1024)}, f32[2048]{0:T(1024)S(1)}, u32[]{:S(2)}) copy-start(f32[2048]{0:T(1024)S(1)} %get-tuple-element.78) | copy-start | bytes 24580
  114.8 9.2 %copy-start.40 = (f32[2048]{0:T(1024)}, f32[2048]{0:T(1024)S(1)}, u32[]{:S(2)}) copy-start(f32[2048]{0:T(1024)S(1)} %get-tuple-element.79) | copy-start | bytes 24580
  114.9 9.2 %copy-start.42 = (f32[2048]{0:T(1024)}, f32[2048]{0:T(1024)S(1)}, u32[]{:S(2)}) copy-start(f32[2048]{0:T(1024)S(1)} %get-tuple-element.80) | copy-start | bytes 24580
  114.9 9.2 %copy-start.44 = (f32[2048]{0:T(1024)}, f32[2048]{0:T(1024)S(1)}, u32[]{:S(2)}) copy-start(f32[2048]{0:T(1024)S(1)} %get-tuple-element.81) | copy-start | bytes 24580
  114.9 9.2 %copy-start.46 = (f32[2048]{0:T(1024)}, f32[2048]{0:T(1024)S(1)}, u32[]{:S(2)}) copy-start(f32[2048]{0:T(1024)S(1)} %get-tuple-element.82) | copy-start | bytes 24580
  114.9 9.2 %copy-start.48 = (f32[2048]{0:T(1024)}, f32[2048]{0:T(1024)S(1)}, u32[]{:S(2)}) copy-start(f32[2048]{0:T(1024)S(1)} %get-tuple-element.83) | copy-start | bytes 24580
  114.9 9.2 %copy-start.50 = (f32[2048]{0:T(1024)}, f32[2048]{0:T(1024)S(1)}, u32[]{:S(2)}) copy-start(f32[2048]{0:T(1024)S(1)} %get-tuple-element.84) | copy-start | bytes 24580
  114.9 9.2 %copy-start.52 = (f32[2048]{0:T(1024)}, f32[2048]{0:T(1024)S(1)}, u32[]{:S(2)}) copy-start(f32[2048]{0:T(1024)S(1)} %get-tuple-element.85) | copy-start | bytes 24580
  114.9 9.2 %copy-start.54 = (f32[2048]{0:T(1024)}, f32[2048]{0:T(1024)S(1)}, u32[]{:S(2)}) copy-start(f32[2048]{0:T(1024)S(1)} %get-tuple-element.86) | copy-start | bytes 24580
  114.9 9.2 %copy-start.56 = (f32[2048]{0:T(1024)}, f32[2048]{0:T(1024)S(1)}, u32[]{:S(2)}) copy-start(f32[2048]{0:T(1024)S(1)} %get-tuple-element.87) | copy-start | bytes 24580
  114.9 7.4 %copy-start.15 = (bf16[4352,256]{1,0:T(8,128)(2,1)S(1)}, bf16[4352,256]{1,0:T(8,128)(2,1)}, u32[]{:S(2)}) copy-start(bf16[4352,256]{1,0:T(8,128)(2,1)} %all-gather.10.cloned.1.call-done) | copy-start | bytes 6684676
  121.5 48.1 %copy-start.58 = (f32[2048]{0:T(1024)}, f32[2048]{0:T(1024)S(1)}, u32[]{:S(2)}) copy-start(f32[2048]{0:T(1024)S(1)} %get-tuple-element.88) | copy-start | bytes 24580
  121.5 48.1 %copy-start.60 = (f32[2048]{0:T(1024)}, f32[2048]{0:T(1024)S(1)}, u32[]{:S(2)}) copy-start(f32[2048]{0:T(1024)S(1)} %get-tuple-element.89) | copy-start | bytes 24580
  121.5 48.1 %copy-start.62 = (f32[2048]{0:T(1024)}, f32[2048]{0:T(1024)S(1)}, u32[]{:S(2)}) copy-start(f32[2048]{0:T(1024)S(1)} %get-tuple-element.90) | copy-start | bytes 24580
  121.5 48.1 %copy-start.64 = (f32[2048]{0:T(1024)}, f32[2048]{0:T(1024)S(1)}, u32[]{:S(2)}) copy-start(f32[2048]{0:T(1024)S(1)} %get-tuple-element.91) | copy-start | bytes 24580
  121.6 48.1 %copy-start.66 = (f32[2048]{0:T(1024)}, f32[2048]{0:T(1024)S(1)}, u32[]{:S(2)}) copy-start(f32[2048]{0:T(1024)S(1)} %get-tuple-element.92) | copy-start | bytes 24580
  121.6 48.1 %copy-start.68 = (f32[2048]{0:T(1024)}, f32[2048]{0:T(1024)S(1)}, u32[]{:S(2)}) copy-start(f32[2048]{0:T(1024)S(1)} %get-tuple-element.93) | copy-start | bytes 24580
  121.6 48.1 %copy-start.70 = (f32[2048]{0:T(1024)}, f32[2048]{0:T(1024)S(1)}, u32[]{:S(2)}) copy-start(f32[2048]{0:T(1024)S(1)} %get-tuple-element.94) | copy-start | bytes 24580
  121.6 48.1 %copy-start.72 = (f32[2048]{0:T(1024)}, f32[2048]{0:T(1024)S(1)}, u32[]{:S(2)}) copy-start(f32[2048]{0:T(1024)S(1)} %get-tuple-element.95) | copy-start | bytes 24580
  121.6 48.1 %copy-start.74 = (f32[2048]{0:T(1024)}, f32[2048]{0:T(1024)S(1)}, u32[]{:S(2)}) copy-start(f32[2048]{0:T(1024)S(1)} %get-tuple-element.96) | copy-start | bytes 24580
  121.6 48.1 %copy-start.76 = (f32[2048]{0:T(1024)}, f32[2048]{0:T(1024)S(1)}, u32[]{:S(2)}) copy-start(f32[2048]{0:T(1024)S(1)} %get-tuple-element.97) | copy-start | bytes 24580
  121.6 48.1 %copy-start.78 = (f32[2048]{0:T(1024)}, f32[2048]{0:T(1024)S(1)}, u32[]{:S(2)}) copy-start(f32[2048]{0:T(1024)S(1)} %get-tuple-element.98) | copy-start | bytes 24580
  121.6 48.1 %copy-start.80 = (f32[2048]{0:T(1024)}, f32[2048]{0:T(1024)S(1)}, u32[]{:S(2)}) copy-start(f32[2048]{0:T(1024)S(1)} %get-tuple-element.99) | copy-start | bytes 24580
  124.2 46.0 %copy-start.16 = (bf16[1,384,2048]{2,1,0:T(8,128)(2,1)S(1)}, bf16[1,384,2048]{2,1,0:T(8,128)(2,1)}, u32[]{:S(2)}) copy-start(bf16[1,384,2048]{2,1,0:T(8,128)(2,1)} %param.19) | copy-start | bytes 4718596
  169.7 4.4 copy-start.6
  174.2 20.4 %copy-start.5 = (bf16[384,2048]{1,0:T(8,128)(2,1)S(1)}, bf16[384,2048]{1,0:T(8,128)(2,1)}, u32[]{:S(2)}) copy-start(bf16[384,2048]{1,0:T(8,128)(2,1)} %copy-done.4) | copy-start | bytes 4718596
  194.6 19.5 %copy-start.7 = (bf16[384,2048]{1,0:T(8,128)(2,1)}, bf16[384,2048]{1,0:T(8,128)(2,1)S(1)}, u32[]{:S(2)}) copy-start(bf16[384,2048]{1,0:T(8,128)(2,1)S(1)} %get-tuple-element.102) | copy-start | bytes 4718596
  233.3 2.2 copy-start.20
  233.3 189.4 %all-gather.12.cloned.1.call-start = ((), (), s32[]{:S(2)}) async-start(), calls=%async_computation.5 | async-start | bytes 3686400 | tf_op jit(solution)/shard_map/all_gather | solution.py:210
  235.5 2.6 copy-start.10
  235.5 10.2 %copy-start.13 = (bf16[3072,256]{0,1:T(8,128)(2,1)}, bf16[3072,256]{0,1:T(8,128)(2,1)S(1)}, u32[]{:S(2)}) copy-start(bf16[3072,256]{0,1:T(8,128)(2,1)S(1)} %get-tuple-element.110) | copy-start | bytes 4718596
  238.2 4.4 copy-start.3
  257.2 296.5 %reduce-scatter.5.cloned.1.call-start = ((), (), s32[]{:S(2)}) async-start(), calls=%async_computation.3 | async-start | bytes 4325376 | tf_op jit(solution)/shard_map/reduce_scatter | solution.py:105
  262.2 9.6 %collective-permute-start.3 = (bf16[15,2048]{1,0:T(8,128)(2,1)}, bf16[15,2048]{1,0:T(8,128)(2,1)}, u32[]{:S(2)}, u32[]{:S(2)}) collective-permute-start(bf16[15,2048]{1,0:T(8,128)(2,1)} %get-tuple-element.113), channel_id=1, source_target_pairs={{0,1},{1,2},{2,3},{3,4},{4,5},{5,6},{6,7},{8,9},{9,10},{10,11},{11... | collective-permute-start | bytes 184328 | tf_op jit(solution)/shard_map/ppermute | solution.py:28
  266.7 6.5 %collective-permute-start.2 = (bf16[15,2048]{1,0:T(8,128)(2,1)}, bf16[15,2048]{1,0:T(8,128)(2,1)}, u32[]{:S(2)}, u32[]{:S(2)}) collective-permute-start(bf16[15,2048]{1,0:T(8,128)(2,1)} %get-tuple-element.112), channel_id=1, source_target_pairs={{1,0},{2,1},{3,2},{4,3},{5,4},{6,5},{7,6},{9,8},{10,9},{11,10},{12... | collective-permute-start | bytes 184328 | tf_op jit(solution)/shard_map/ppermute | solution.py:30
  271.4 1.9 copy-start.29
  271.7 325.6 %all-gather.14.cloned.1.call-start = ((), (), s32[]{:S(2)}) async-start(), calls=%async_computation.6 | async-start | bytes 1253376 | tf_op jit(solution)/shard_map/all_gather | solution.py:115
  271.7 34.8 %copy-start.9 = (bf16[1,384,4096]{2,1,0:T(8,128)(2,1)S(1)}, bf16[1,384,4096]{2,1,0:T(8,128)(2,1)}, u32[]{:S(2)}) copy-start(bf16[1,384,4096]{2,1,0:T(8,128)(2,1)} %param.16) | copy-start | bytes 9437188
  307.6 39.0 %copy-start.11 = (bf16[3072,256]{0,1:T(8,128)(2,1)S(1)}, bf16[3072,256]{0,1:T(8,128)(2,1)}, u32[]{:S(2)}) copy-start(bf16[3072,256]{0,1:T(8,128)(2,1)} %copy-done.10) | copy-start | bytes 4718596
  307.7 39.0 %copy-start.14 = (bf16[3072,256]{0,1:T(8,128)(2,1)S(1)}, bf16[3072,256]{0,1:T(8,128)(2,1)}, u32[]{:S(2)}) copy-start(bf16[3072,256]{0,1:T(8,128)(2,1)} %copy-done.13) | copy-start | bytes 4718596
  307.7 39.0 %copy-start.84 = (f32[2,384]{1,0:T(2,128)S(1)}, f32[2,384]{1,0:T(2,128)}, u32[]{:S(2)}) copy-start(f32[2,384]{1,0:T(2,128)} %copy-done.83) | copy-start | bytes 9220
  426.6 1.9 copy-start.12
  426.6 5.5 copy-start.21
  432.2 124.0 %copy-start.17 = (bf16[3072,256]{0,1:T(8,128)(2,1)S(1)}, bf16[3072,256]{0,1:T(8,128)(2,1)}, u32[]{:S(2)}) copy-start(bf16[3072,256]{0,1:T(8,128)(2,1)} %copy.124) | copy-start | bytes 4718596
  432.2 124.0 %copy-start.87 = (pred[384]{0:T(512)(128)(4,1)S(1)}, pred[384]{0:T(512)(128)(4,1)}, u32[]{:S(2)}) copy-start(pred[384]{0:T(512)(128)(4,1)} %get-tuple-element.107) | copy-start | bytes 1156
  565.4 35.3 %copy-start.1 = (bf16[1,384,4096]{2,1,0:T(8,128)(2,1)S(1)}, bf16[1,384,4096]{2,1,0:T(8,128)(2,1)}, u32[]{:S(2)}) copy-start(bf16[1,384,4096]{2,1,0:T(8,128)(2,1)} %param.15) | copy-start | bytes 9437188
  (34 other events, 61.0 us)
Sparse Core Ops, SparseCore 0:
  11.3 80.6 all-gather.9
  93.8 73.0 all-gather.7
  233.4 112.3 reduce-scatter.6
  347.4 75.2 all-gather.11
  426.7 126.9 reduce-scatter.4
  555.5 41.6 all-gather.13
